TPU v7x, 256 devices: a whole 4x4x8 slice. The times are simulated.
256 devices in a mesh: replica: 8 (over y, core), fsdp: 32 (over x, z).
Axes of the slice: x: 4, y: 4, z: 8, core: 2. Of those that a mesh axis runs over, the one named last changes fastest.
Arguments:
- anchor_params: bfloat16 [24, 512, 4096], P(None, 'fsdp')
- replica_params: bfloat16 [8, 24, 512, 4096], P('replica', None, 'fsdp')
- projection: bfloat16 [4096, 384], replicated
- momentum: float32 [24, 512, 384], P(None, 'fsdp'), may hold values from -1.8 to 1.8
- rate_table: float32 [4, 6], replicated, may hold values from 0.1 to 1
- owner_list: int32 [24], replicated, may hold values from 0 to 31, as said below
- layer_kind: int32 [24, 2], replicated, may hold values from 0 to 5, as said below
Outputs:
- new_params: bfloat16 [24, 512, 4096], P(None, 'fsdp')
- new_momentum: float32 [24, 512, 384], P(None, 'fsdp')
Inputs may be any that keep to these rules, and one draw needn't show every extreme that they name: `owner_list`: no fsdp index is named more than 2 times, and in every draw some index is named exactly 2 times. `layer_kind`: column 0 is a layer, column 1 a kind below 6; each layer has 6 rows, and no two rows are equal.
All inputs are finite; a program needn't handle non-finite values.
Results may differ from a plain program's by a relative error of at most 0.0055.
Values may be sent and summed in bfloat16 or wider, within the bound.
No kernel may reach another device: no remote copies, remote signals or barrier semaphores. Data moves between devices by JAX's collectives and lax.ppermute only.
A program may use at most 128 MiB of HBM per device.

v0:
```python
import jax
import jax.numpy as jnp
from jax import lax
from jax.sharding import PartitionSpec as P

OUTER_MOMENTUM = 0.9
EPSILON = 1e-06


def local(anchor_params, replica_params, projection, momentum, rate_table, owner_list, layer_kind):
    matrices, rows_dev, model_width = anchor_params.shape
    rank_dim = projection.shape[1]
    all_rows = rows_dev * lax.axis_size("fsdp")
    highest = lax.Precision.HIGHEST
    pseudo_grad = (
        anchor_params.astype(jnp.float32) - replica_params[0].astype(jnp.float32)
    ).astype(jnp.bfloat16)
    compressed = jnp.dot(
        pseudo_grad.reshape(matrices * rows_dev, model_width),
        projection,
        preferred_element_type=jnp.float32,
    )
    summed = lax.psum(compressed.reshape(matrices, rows_dev, rank_dim), "replica")
    outer_grad = summed / lax.axis_size("replica")
    new_momentum = OUTER_MOMENTUM * momentum + outer_grad
    outer_step = outer_grad + OUTER_MOMENTUM * new_momentum
    squares = lax.psum(jnp.sum(outer_step * outer_step, axis=(1, 2)), "fsdp")
    same_group = (owner_list[:, None] == owner_list[None, :]).astype(jnp.float32)
    group_squares = jnp.dot(same_group, squares, precision=highest)
    group_count = jnp.sum(same_group, axis=1)
    scaling = lax.rsqrt(group_squares / (group_count * (all_rows * rank_dim)) + EPSILON)
    outer_rate = rate_table[layer_kind[:, 0], layer_kind[:, 1]]
    direction = (outer_step * (outer_rate * scaling)[:, None, None]).astype(jnp.bfloat16)
    update = lax.dot_general(
        direction.reshape(matrices * rows_dev, rank_dim),
        projection,
        (((1,), (1,)), ((), ())),
        preferred_element_type=jnp.float32,
    ).astype(jnp.bfloat16)
    new_params = (
        anchor_params.astype(jnp.float32)
        - update.reshape(matrices, rows_dev, model_width).astype(jnp.float32)
    ).astype(jnp.bfloat16)
    return (new_params, new_momentum)


def solution(mesh):
    placed = (
        P(None, "fsdp", None),
        P("replica", None, "fsdp", None),
        P(),
        P(None, "fsdp", None),
        P(),
        P(),
        P(),
    )
    return jax.shard_map(
        local,
        mesh=mesh,
        in_specs=placed,
        out_specs=(P(None, "fsdp", None), P(None, "fsdp", None)),
        check_vma=False,
    )
```

profile of v0, /device:TPU:0, one launch (start us, length us, event | category | flops | bytes accessed | tf_op | source)
XLA Modules:
  0.0 172.9 jit_solution(15849342084656338026)
XLA Ops:
  7.2 0.0 copy-start
  7.2 0.0 copy-start.3
  7.2 0.0 copy-start.1
  7.2 0.0 copy-start.4
  7.2 0.0 all-reduce.2.cloned.1.call-start
  7.3 1.8 %copy-done = bf16[4096,384]{1,0:T(8,128)(2,1)S(1)} copy-done((bf16[4096,384]{1,0:T(8,128)(2,1)S(1)}, bf16[4096,384]{1,0:T(8,128)(2,1)}, u32[]{:S(2)}) %copy-start) | copy-done | bytes 3145752
  9.1 5.5 %fusion.2 = f32[24,16,384]{2,1,0:T(8,128)} fusion(bf16[24,16,4096]{2,1,0:T(8,128)(2,1)} %param.7, bf16[1,24,16,4096]{3,2,1,0:T(8,128)(2,1)} %param.8, bf16[4096,384]{1,0:T(8,128)(2,1)S(1)} %copy-done), kind=kOutput, calls=%fused_computation.6 | convolution fusion | flops 1214251008 | bytes 10027008 | tf_op jit(solution)/shard_map/dot_general | solution.py:18
  14.5 0.0 all-reduce.2.cloned.1.call-update
  14.5 0.0 copy-done.3
  14.6 0.0 copy-done.1
  14.6 0.8 gather_fusion
  15.4 0.0 copy-done.4
  15.4 0.2 fusion.11
  15.6 66.8 %all-reduce.2.cloned.1.call-done = f32[24,16,384]{2,1,0:T(8,128)} async-done(((f32[24,16,384]{2,1,0:T(8,128)}), f32[24,16,384]{2,1,0:T(8,128)}) %all-reduce.2.cloned.1.call-update) | async-done | bytes 589840 | tf_op jit(solution)/shard_map/psum | solution.py:23
  82.4 2.2 %multiply_reduce_fusion = (f32[24]{0:T(128)S(1)}, f32[24,16,384]{2,1,0:T(8,128)}) fusion(f32[24,16,384]{2,1,0:T(8,128)} %all-reduce.2.cloned.1.call-done, f32[24,16,384]{2,1,0:T(8,128)} %param.10), kind=kLoop, calls=%fused_computation.15 | loop fusion | flops 1032168 | bytes 1769568 | tf_op jit(solution)/shard_map/reduce_sum | solution.py:27
  84.7 75.0 %psum.15 = f32[24]{0:T(128)S(1)} all-reduce(f32[24]{0:T(128)S(1)} %get-tuple-element.2), channel_id=1, replica_groups=mesh['replica'=8,'fsdp'=32] {'fsdp'}, use_global_device_ids=true, to_apply=%region_2.0 | all-reduce | flops 24 | bytes 192 | tf_op jit(solution)/shard_map/psum | solution.py:27
  159.7 0.2 fusion.9
  159.9 1.4 multiply_convert_fusion
  161.3 0.0 copy-start.2
  161.3 1.8 %convolution_convert_fusion = bf16[384,4096]{1,0:T(8,128)(2,1)S(1)} fusion(bf16[384,384]{1,0:T(8,128)(2,1)S(1)} %bitcast.30, bf16[4096,384]{1,0:T(8,128)(2,1)S(1)} %copy-done), kind=kOutput, calls=%fused_computation.5 | convolution fusion | flops 1209532416 | bytes 6586368 | tf_op jit(solution)/shard_map/dot_general | solution.py:34
  163.1 0.0 copy-done.2
  163.2 2.9 %fusion.1 = bf16[24,16,4096]{2,1,0:T(8,128)(2,1)} fusion(bf16[24,16,4096]{2,1,0:T(8,128)(2,1)S(1)} %copy-done.2, bf16[24,16,4096]{2,1,0:T(8,128)(2,1)S(1)} %bitcast.29), kind=kLoop, calls=%fused_computation.4 | loop fusion | flops 6291456 | bytes 9437184 | tf_op jit(solution)/shard_map/convert_element_type | solution.py:43
  (1 shorter events, 0.0 us)
Async XLA Ops:
  7.2 1.9 %copy-start = (bf16[4096,384]{1,0:T(8,128)(2,1)S(1)}, bf16[4096,384]{1,0:T(8,128)(2,1)}, u32[]{:S(2)}) copy-start(bf16[4096,384]{1,0:T(8,128)(2,1)} %param.9) | copy-start | bytes 9437188
  7.2 7.4 %copy-start.3 = (s32[24,2]{0,1:T(2,128)S(1)}, s32[24,2]{0,1:T(2,128)}, u32[]{:S(2)}) copy-start(s32[24,2]{0,1:T(2,128)} %param.13) | copy-start | bytes 580
  7.2 7.4 %copy-start.1 = (f32[4,6]{1,0:T(4,128)S(1)}, f32[4,6]{1,0:T(4,128)}, u32[]{:S(2)}) copy-start(f32[4,6]{1,0:T(4,128)} %param.11) | copy-start | bytes 292
  7.2 8.2 %copy-start.4 = (s32[24]{0:T(128)S(1)}, s32[24]{0:T(128)}, u32[]{:S(2)}) copy-start(s32[24]{0:T(128)} %param.12) | copy-start | bytes 292
  7.2 75.2 %all-reduce.2.cloned.1.call-start = ((), (), s32[]{:S(2)}) async-start(), calls=%async_computation | async-start | bytes 1179648 | tf_op jit(solution)/shard_map/psum | solution.py:23
  161.3 1.9 %copy-start.2 = (bf16[24,16,4096]{2,1,0:T(8,128)(2,1)S(1)}, bf16[24,16,4096]{2,1,0:T(8,128)(2,1)}, u32[]{:S(2)}) copy-start(bf16[24,16,4096]{2,1,0:T(8,128)(2,1)} %param.7) | copy-start | bytes 9437188
Sparse Core Ops, SparseCore 0:
  14.7 67.7 all-reduce.1
where the time goes:
time: 173 us
  blocking collectives  75 us (43%)
  waiting for transfers between devices  66.8 us (39%)
  between operations  14.1 us (8%)
  matrix products  7.48 us (4%)
  other arithmetic  6.67 us (4%)
  local copies, waits for them, and re-layouts  2.71 us (2%)
    psum x1, blocking collectives, local(): squares = lax.psum(jnp.sum(outer_step * outer_step, axis=(1, 2)), 'fsdp')  75 us
    psum x1, waiting for transfers between devices, local(): lax.psum(compressed.reshape(matrices, rows_dev, rank_dim), 'replica')  66.8 us
    dot_general x1, matrix products, local(): jnp.dot(pseudo_grad.reshape(matrices * rows_dev, model_width), projection...  5.45 us
  transfers between devices with their start and end apart: 1, of which 1 were waited for; matrix products, arithmetic and copies ran while one was open for 1% of the time, Pallas kernels for 0%

commit v1 on v0

--- a/solution.py
+++ b/solution.py
@@ -20,7 +20,9 @@
         projection,
         preferred_element_type=jnp.float32,
     )
-    summed = lax.psum(compressed.reshape(matrices, rows_dev, rank_dim), "replica")
+    summed = jnp.sum(
+        lax.all_gather(compressed.reshape(matrices, rows_dev, rank_dim), "replica"), axis=0
+    )
     outer_grad = summed / lax.axis_size("replica")
     new_momentum = OUTER_MOMENTUM * momentum + outer_grad
     outer_step = outer_grad + OUTER_MOMENTUM * new_momentum

time: 173 us -> 148 us (0.86)
  waiting for transfers between devices: 66.8 us -> 37.2 us
  other arithmetic: 6.67 us -> 10.2 us
    psum x1 -> x0, waiting for transfers between devices: 66.8 us -> none  [local(): lax.psum(compressed.reshape(matrices, rows_dev, rank_dim), 'replica')]
    all_gather x0 -> x1, waiting for transfers between devices: none -> 37.2 us  [local(): lax.all_gather(compressed.reshape(matrices, rows_dev, rank_dim), 'replica')]
    reduce_sum x0 -> x1, other arithmetic: none -> 3.51 us  [local(): jnp.sum(lax.all_gather(compressed.reshape(matrices, rows_dev, rank_dim),...]
where the time goes in v1:
time: 148 us; the launch traced here: 147 us
  blocking collectives  75 us (51%)
  waiting for transfers between devices  37.2 us (25%)
  between operations  14.1 us (10%)
  other arithmetic  10.2 us (7%)
  matrix products  7.48 us (5%)
  local copies, waits for them, and re-layouts  2.71 us (2%)
    psum x1, blocking collectives, local(): squares = lax.psum(jnp.sum(outer_step * outer_step, axis=(1, 2)), 'fsdp')  75 us
    all_gather x1, waiting for transfers between devices, local(): lax.all_gather(compressed.reshape(matrices, rows_dev, rank_dim), 'replica')  37.2 us
    dot_general x1, matrix products, local(): jnp.dot(pseudo_grad.reshape(matrices * rows_dev, model_width), projection...  5.45 us
    reduce_sum x1, other arithmetic, local(): jnp.sum(lax.all_gather(compressed.reshape(matrices, rows_dev, rank_dim),...  3.51 us
  transfers between devices with their start and end apart: 1, of which 1 were waited for; matrix products, arithmetic and copies ran while one was open for 1% of the time, Pallas kernels for 0%

profile of v1, /device:TPU:0, one launch (start us, length us, event | category | flops | bytes accessed | tf_op | source)
XLA Modules:
  0.0 146.8 jit_solution(14506026319293707249)
XLA Ops:
  7.2 0.0 copy-start
  7.2 0.0 copy-start.3
  7.2 0.0 copy-start.1
  7.2 0.0 copy-start.4
  7.2 0.0 all-gather.3.cloned.1.call-start
  7.3 1.8 %copy-done = bf16[4096,384]{1,0:T(8,128)(2,1)S(1)} copy-done((bf16[4096,384]{1,0:T(8,128)(2,1)S(1)}, bf16[4096,384]{1,0:T(8,128)(2,1)}, u32[]{:S(2)}) %copy-start) | copy-done | bytes 3145752
  9.1 5.5 %fusion.2 = f32[24,16,384]{2,1,0:T(8,128)} fusion(bf16[24,16,4096]{2,1,0:T(8,128)(2,1)} %param.7, bf16[1,24,16,4096]{3,2,1,0:T(8,128)(2,1)} %param.8, bf16[4096,384]{1,0:T(8,128)(2,1)S(1)} %copy-done), kind=kOutput, calls=%fused_computation.6 | convolution fusion | flops 1214251008 | bytes 10027008 | tf_op jit(solution)/shard_map/dot_general | solution.py:18
  14.5 0.0 all-gather.3.cloned.1.call-update
  14.5 0.0 copy-done.3
  14.6 0.0 copy-done.1
  14.6 0.8 gather_fusion
  15.4 0.0 copy-done.4
  15.4 0.2 fusion.11
  15.6 37.2 %all-gather.3.cloned.1.call-done = f32[192,16,384]{2,1,0:T(8,128)} async-done(((f32[24,16,384]{2,1,0:T(8,128)}), f32[192,16,384]{2,1,0:T(8,128)}) %all-gather.3.cloned.1.call-update) | async-done | bytes 4718608 | tf_op jit(solution)/shard_map/all_gather | solution.py:24
  52.8 3.5 %reduce_sum.27 = f32[24,16,384]{2,1,0:T(8,128)} reduce(f32[8,24,16,384]{3,2,1,0:T(8,128)} %bitcast.30, f32[]{:T(128)} %constant.1.clone.1), dimensions={0}, to_apply=%region_0.0 | reduce | flops 1032192 | bytes 5308420 | tf_op jit(solution)/shard_map/reduce_sum | solution.py:23
  56.3 2.2 %multiply_reduce_fusion = (f32[24]{0:T(128)S(1)}, f32[24,16,384]{2,1,0:T(8,128)}) fusion(f32[24,16,384]{2,1,0:T(8,128)} %reduce_sum.27, f32[24,16,384]{2,1,0:T(8,128)} %param.10), kind=kLoop, calls=%fused_computation.15 | loop fusion | flops 1032168 | bytes 1769568 | tf_op jit(solution)/shard_map/reduce_sum | solution.py:29
  58.5 75.0 %psum.7 = f32[24]{0:T(128)S(1)} all-reduce(f32[24]{0:T(128)S(1)} %get-tuple-element.2), channel_id=1, replica_groups=mesh['replica'=8,'fsdp'=32] {'fsdp'}, use_global_device_ids=true, to_apply=%region_2.0 | all-reduce | flops 24 | bytes 192 | tf_op jit(solution)/shard_map/psum | solution.py:29
  133.6 0.2 fusion.9
  133.8 1.4 multiply_convert_fusion
  135.1 0.0 copy-start.2
  135.2 1.8 %convolution_convert_fusion = bf16[384,4096]{1,0:T(8,128)(2,1)S(1)} fusion(bf16[384,384]{1,0:T(8,128)(2,1)S(1)} %bitcast.32, bf16[4096,384]{1,0:T(8,128)(2,1)S(1)} %copy-done), kind=kOutput, calls=%fused_computation.5 | convolution fusion | flops 1209532416 | bytes 6586368 | tf_op jit(solution)/shard_map/dot_general | solution.py:36
  137.0 0.0 copy-done.2
  137.0 2.9 %fusion.1 = bf16[24,16,4096]{2,1,0:T(8,128)(2,1)} fusion(bf16[24,16,4096]{2,1,0:T(8,128)(2,1)S(1)} %copy-done.2, bf16[24,16,4096]{2,1,0:T(8,128)(2,1)S(1)} %bitcast.31), kind=kLoop, calls=%fused_computation.4 | loop fusion | flops 6291456 | bytes 9437184 | tf_op jit(solution)/shard_map/convert_element_type | solution.py:45
  (1 shorter events, 0.0 us)
Async XLA Ops:
  7.2 1.9 %copy-start = (bf16[4096,384]{1,0:T(8,128)(2,1)S(1)}, bf16[4096,384]{1,0:T(8,128)(2,1)}, u32[]{:S(2)}) copy-start(bf16[4096,384]{1,0:T(8,128)(2,1)} %param.9) | copy-start | bytes 9437188
  7.2 7.4 %copy-start.3 = (s32[24,2]{0,1:T(2,128)S(1)}, s32[24,2]{0,1:T(2,128)}, u32[]{:S(2)}) copy-start(s32[24,2]{0,1:T(2,128)} %param.13) | copy-start | bytes 580
  7.2 7.4 %copy-start.1 = (f32[4,6]{1,0:T(4,128)S(1)}, f32[4,6]{1,0:T(4,128)}, u32[]{:S(2)}) copy-start(f32[4,6]{1,0:T(4,128)} %param.11) | copy-start | bytes 292
  7.2 8.2 %copy-start.4 = (s32[24]{0:T(128)S(1)}, s32[24]{0:T(128)}, u32[]{:S(2)}) copy-start(s32[24]{0:T(128)} %param.12) | copy-start | bytes 292
  7.2 45.6 %all-gather.3.cloned.1.call-start = ((), (), s32[]{:S(2)}) async-start(), calls=%async_computation | async-start | bytes 5308416 | tf_op jit(solution)/shard_map/all_gather | solution.py:24
  135.1 1.9 %copy-start.2 = (bf16[24,16,4096]{2,1,0:T(8,128)(2,1)S(1)}, bf16[24,16,4096]{2,1,0:T(8,128)(2,1)}, u32[]{:S(2)}) copy-start(bf16[24,16,4096]{2,1,0:T(8,128)(2,1)} %param.7) | copy-start | bytes 9437188
Sparse Core Ops, SparseCore 0:
  14.7 38.0 all-gather.2
